TPU v7x, 512 devices: a whole 4x4x16 slice. The times are simulated.
512 devices in a mesh: section: 32 (over z, core), blk: 16 (over y, x).
Axes of the slice: x: 4, y: 4, z: 16, core: 2. Of those that a mesh axis runs over, the one named last changes fastest.
Arguments:
- held_input: bfloat16 [32, 5120, 128], P('section', 'blk'), may hold values from -6 to 6
- fresh_input: bfloat16 [5120, 128], P('blk'), may hold values from -6 to 6
- stashed: bfloat16 [32, 2, 5120, 128], P('section', None, 'blk'), may hold values from -6 to 6
- held_grad: bfloat16 [32, 5120, 128], P('section', 'blk'), may hold values from -6 to 6
- fresh_grad: bfloat16 [5120, 128], P('blk'), may hold values from -6 to 6
- first_up: bfloat16 [32, 2, 128, 6400], P('section', None, 'blk'), may hold values from -1 to 1
- second_up: bfloat16 [32, 2, 160, 16384], P('section', None, 'blk'), may hold values from -0.5 to 0.5
- first_down: bfloat16 [32, 160, 16384], P('section', 'blk'), may hold values from -0.5 to 0.5
- second_down: bfloat16 [32, 128, 6400], P('section', 'blk'), may hold values from -0.5 to 0.5
Outputs:
- passed_output: bfloat16 [32, 5120, 128], P('section', 'blk')
- passed_grad: bfloat16 [32, 5120, 128], P('section', 'blk')
- grad_first_up: bfloat16 [32, 2, 128, 6400], P('section', None, 'blk')
- grad_second_up: bfloat16 [32, 2, 160, 16384], P('section', None, 'blk')
- grad_first_down: bfloat16 [32, 160, 16384], P('section', 'blk')
- grad_second_down: bfloat16 [32, 128, 6400], P('section', 'blk')
All inputs are finite; a program needn't handle non-finite values.
Results may differ from a plain program's by a relative error of at most 0.0095.
Values may be sent and summed in bfloat16 or wider, within the bound.
No kernel may reach another device: no remote copies, remote signals or barrier semaphores. Data moves between devices by JAX's collectives and lax.ppermute only.
A program may use at most 64 MiB of HBM per device.

v0:
```python
import math
import jax
import jax.numpy as jnp
from jax import lax
from jax.sharding import PartitionSpec as P

BLOCK = 128
FIRST_BLOCKS = 128
FIRST_IN = 40
SECOND_BLOCKS = 160
TICKS = 2


def from_behind(value, axis, by):
    length = lax.axis_size(axis)
    pairs = [(i, i + by) for i in range(length) if 0 <= i + by < length]
    return lax.ppermute(value, axis, pairs)


def to_blocks(pieces):
    return lax.all_to_all(pieces, "blk", split_axis=1, concat_axis=0, tiled=True)


def to_features(pieces):
    groups = lax.axis_size("blk")
    r_local, p_all, n = pieces.shape
    p_local = p_all // groups
    grouped = pieces.reshape(r_local, groups, p_local, n).transpose(1, 0, 2, 3)
    arrived = lax.all_to_all(grouped, "blk", split_axis=0, concat_axis=0, tiled=True)
    return arrived.reshape(groups * r_local, p_local, n)


def spread_of(values, up_first):
    return jnp.einsum(
        "pqt,gpqr->prgt", values, up_first, preferred_element_type=jnp.float32
    ).astype(jnp.bfloat16)


def lowered_grad_of(grads, down_second):
    return jnp.einsum(
        "pqt,prq->prt", grads, down_second, preferred_element_type=jnp.float32
    ).astype(jnp.bfloat16)


def forward_middle(spread_r, up_second, down_first):
    mixed = jnp.einsum("prgt,grpo->grot", spread_r, up_second, preferred_element_type=jnp.float32)
    hidden = (jax.nn.silu(mixed[0]) * mixed[1]).astype(jnp.bfloat16)
    lowered = jnp.einsum(
        "rot,rop->rpt", hidden, down_first, preferred_element_type=jnp.float32
    ).astype(jnp.bfloat16)
    return (mixed, hidden, lowered)


def backward_middle(mixed, grad_lowered_r, up_second, down_first):
    grad_hidden = jnp.einsum(
        "prt,rop->rot", grad_lowered_r, down_first, preferred_element_type=jnp.float32
    )
    sigmoid_gate = jax.nn.sigmoid(mixed[0])
    slope = sigmoid_gate * (1.0 + mixed[0] * (1.0 - sigmoid_gate))
    grad_mixed = jnp.stack(
        [grad_hidden * mixed[1] * slope, grad_hidden * mixed[0] * sigmoid_gate]
    ).astype(jnp.bfloat16)
    grad_spread = jnp.einsum(
        "grot,grpo->grpt", grad_mixed, up_second, preferred_element_type=jnp.float32
    ).astype(jnp.bfloat16)
    return (grad_mixed, grad_spread)


def output_of(values, lowered_p, down_second):
    added = jnp.einsum("rpt,prq->pqt", lowered_p, down_second, preferred_element_type=jnp.float32)
    return (values.astype(jnp.float32) + added).astype(jnp.bfloat16)


def input_grad_of(grads, grad_spread_p, up_first):
    added = jnp.einsum(
        "rpgt,gpqr->pqt", grad_spread_p, up_first, preferred_element_type=jnp.float32
    )
    return (grads.astype(jnp.float32) + added).astype(jnp.bfloat16)


def shards(
    held_input,
    fresh_input,
    stashed,
    held_grad,
    fresh_grad,
    first_up,
    second_up,
    first_down,
    second_down,
):
    feature_blocks = first_up.shape[2]
    hidden_blocks = second_up.shape[2]
    tokens = held_input.shape[2]
    up_first = first_up[0].reshape(2, feature_blocks, FIRST_IN, SECOND_BLOCKS)
    up_second = second_up[0].reshape(2, hidden_blocks, FIRST_BLOCKS, BLOCK)
    down_first = first_down[0].reshape(hidden_blocks, BLOCK, FIRST_BLOCKS)
    down_second = second_down[0].reshape(feature_blocks, SECOND_BLOCKS, FIRST_IN)
    first_inputs = held_input[0].reshape(feature_blocks, FIRST_IN, tokens)
    first_grads = held_grad[0].reshape(feature_blocks, FIRST_IN, tokens)
    stash_views = [stashed[0, k].reshape(feature_blocks, FIRST_IN, tokens) for k in range(TICKS)]
    section_pos = lax.axis_index("section")
    last_section = lax.axis_size("section") - 1
    t = tokens
    values_a = jnp.concatenate([first_inputs] + stash_views, axis=2)
    spread_a = spread_of(values_a, up_first)
    glow_1 = lowered_grad_of(first_grads, down_second)
    payload = jnp.concatenate(
        [spread_a.reshape(feature_blocks, SECOND_BLOCKS, 2 * 3 * t), glow_1], axis=2
    )
    arrived = to_blocks(payload)
    spread_ar = arrived[:, :, : 6 * t].reshape(FIRST_BLOCKS, hidden_blocks, 2, 3 * t)
    glow_1r = arrived[:, :, 6 * t :]
    mixed_a, hidden_a, lowered_a = forward_middle(spread_ar, up_second, down_first)
    gmix_1, gspread_1 = backward_middle(mixed_a[:, :, :, t : 2 * t], glow_1r, up_second, down_first)
    payload = jnp.concatenate([lowered_a, gspread_1[0], gspread_1[1]], axis=2)
    back = to_features(payload)
    lowered_ap = back[:, :, : 3 * t]
    gspread_1p = back[:, :, 3 * t :].reshape(SECOND_BLOCKS, feature_blocks, 2, t)
    outputs = output_of(first_inputs, lowered_ap[:, :, :t], down_second)
    backward = input_grad_of(first_grads, gspread_1p, up_first)
    moved_forward = from_behind(outputs, "section", 1)
    inputs = jnp.where(
        section_pos == 0, fresh_input.reshape(feature_blocks, FIRST_IN, tokens), moved_forward
    )
    moved_backward = from_behind(backward, "section", -1)
    grads = jnp.where(
        section_pos == last_section,
        fresh_grad.reshape(feature_blocks, FIRST_IN, tokens),
        moved_backward,
    )
    spread_b = spread_of(inputs, up_first)
    glow_2 = lowered_grad_of(grads, down_second)
    payload = jnp.concatenate(
        [spread_b.reshape(feature_blocks, SECOND_BLOCKS, 2 * t), glow_2], axis=2
    )
    arrived = to_blocks(payload)
    spread_br = arrived[:, :, : 2 * t].reshape(FIRST_BLOCKS, hidden_blocks, 2, t)
    glow_2r = arrived[:, :, 2 * t :]
    _, _, lowered_b = forward_middle(spread_br, up_second, down_first)
    gmix_2, gspread_2 = backward_middle(mixed_a[:, :, :, 2 * t :], glow_2r, up_second, down_first)
    payload = jnp.concatenate([lowered_b, gspread_2[0], gspread_2[1]], axis=2)
    back = to_features(payload)
    lowered_bp = back[:, :, :t]
    gspread_2p = back[:, :, t:].reshape(SECOND_BLOCKS, feature_blocks, 2, t)
    outputs = output_of(inputs, lowered_bp, down_second)
    backward = input_grad_of(grads, gspread_2p, up_first)
    stash_both = jnp.concatenate(stash_views, axis=2)
    gspread_both = jnp.concatenate([gspread_1p, gspread_2p], axis=3)
    spread_both = spread_ar[:, :, :, t:]
    gmix_both = jnp.concatenate([gmix_1, gmix_2], axis=3)
    hidden_both = hidden_a[:, :, t:]
    glow_both = jnp.concatenate([glow_1r, glow_2r], axis=2)
    lowered_both = lowered_ap[:, :, t:]
    grads_both = jnp.concatenate([first_grads, grads], axis=2)
    total_first_up = jnp.einsum(
        "pqt,rpgt->gpqr", stash_both, gspread_both, preferred_element_type=jnp.float32
    )
    total_second_up = jnp.einsum(
        "prgt,grot->grpo", spread_both, gmix_both, preferred_element_type=jnp.float32
    )
    total_first_down = jnp.einsum(
        "rot,prt->rop", hidden_both, glow_both, preferred_element_type=jnp.float32
    )
    total_second_down = jnp.einsum(
        "rpt,pqt->prq", lowered_both, grads_both, preferred_element_type=jnp.float32
    )
    factor = 1.0 / math.sqrt(TICKS * tokens)
    return (
        outputs.reshape(held_input.shape),
        backward.reshape(held_grad.shape),
        (total_first_up * factor).astype(jnp.bfloat16).reshape(first_up.shape),
        (total_second_up * factor).astype(jnp.bfloat16).reshape(second_up.shape),
        (total_first_down * factor).astype(jnp.bfloat16).reshape(first_down.shape),
        (total_second_down * factor).astype(jnp.bfloat16).reshape(second_down.shape),
    )


def solution(mesh):
    return jax.shard_map(
        shards,
        mesh=mesh,
        in_specs=(
            P("section", "blk", None),
            P("blk", None),
            P("section", None, "blk", None),
            P("section", "blk", None),
            P("blk", None),
            P("section", None, "blk", None),
            P("section", None, "blk", None),
            P("section", "blk", None),
            P("section", "blk", None),
        ),
        out_specs=(
            P("section", "blk", None),
            P("section", "blk", None),
            P("section", None, "blk", None),
            P("section", None, "blk", None),
            P("section", "blk", None),
            P("section", "blk", None),
        ),
        check_vma=False,
    )
```

profile of v0, /device:TPU:224, one launch (start us, length us, event | category | flops | bytes accessed | tf_op | source)
XLA Modules:
  0.0 168.3 jit_solution(5044812806253064722)
XLA Ops:
  0.6 0.9 fusion.103
  1.6 1.4 reshape_squeeze.27
  3.0 1.6 reshape_squeeze.28
  4.5 1.6 convert_bitcast_fusion
  6.4 0.7 copy-done.27
  7.0 0.2 convolution_convert_fusion.5
  7.5 2.1 %copy.143 = bf16[8,160,896]{2,0,1:T(8,128)(2,1)} copy(bf16[8,160,896]{2,1,0:T(8,128)(2,1)S(1)} %pad_maximum_fusion) | data formatting | bytes 4587520 | tf_op jit(solution)/shard_map/concatenate | solution.py:108
  9.6 7.2 %all-to-all-start = ((bf16[8,160,896]{2,0,1:T(8,128)(2,1)}), bf16[8,160,896]{2,0,1:T(8,128)(2,1)S(1)}, u32[]{:S(2)}, u32[]{:S(2)}) async-start(bf16[8,160,896]{2,0,1:T(8,128)(2,1)} %copy.143), calls=%async_computation | async-start | bytes 4587520 | tf_op jit(solution)/shard_map/all_to_all | solution.py:21
  16.8 0.9 copy.218
  17.7 2.3 %reshape_squeeze.30 = bf16[2,10,128,128]{3,2,0,1:T(8,128)(2,1)S(1)} reshape(bf16[1,2,10,16384]{3,1,2,0:T(2,128)(2,1)} %param.15) | data formatting | bytes 1310720 | tf_op jit(solution)/shard_map/reshape;squeeze | solution.py:96
  20.0 31.3 %all-to-all-done = bf16[8,160,896]{2,0,1:T(8,128)(2,1)S(1)} async-done(((bf16[8,160,896]{2,0,1:T(8,128)(2,1)}), bf16[8,160,896]{2,0,1:T(8,128)(2,1)S(1)}, u32[]{:S(2)}, u32[]{:S(2)}) %all-to-all-start) | async-done | bytes 2293792 | tf_op jit(solution)/shard_map/all_to_all | solution.py:21
  51.3 1.4 copy-done.1
  52.8 2.0 %copy.262 = bf16[16,8,10,896]{3,1,0,2:T(8,128)(2,1)S(1)} copy(bf16[16,8,10,896]{3,1,2,0:T(8,128)(2,1)} %bitcast.213) | data formatting | bytes 4587520 | tf_op jit(solution)/shard_map/all_to_all | solution.py:21
  54.7 1.5 slice.113
  56.2 4.0 %copy.145 = bf16[128,10,768]{0,2,1:T(8,128)(2,1)} copy(bf16[128,10,768]{2,0,1:T(8,128)(2,1)} %slice.113) | data formatting | bytes 3932160 | tf_op jit(solution)/shard_map/slice | solution.py:112
  60.2 2.2 %convolution_bitcast_fusion = f32[2,10,128,384]{2,3,1,0:T(8,128)S(1)} fusion(bf16[128,10,2,384]{0,3,2,1:T(8,128)(2,1)} %bitcast.214, bf16[2,10,128,128]{3,2,0,1:T(8,128)(2,1)S(1)} %reshape_squeeze.30), kind=kOutput, calls=%fused_computation.2 | convolution fusion | flops 251658240 | bytes 6553600 | tf_op jit(solution)/shard_map/prgt,grpo->grot/dot_general | solution.py:46
  62.4 0.5 fusion.1
  62.9 1.3 copy-done
  64.3 0.5 fusion.66
  64.8 0.6 fusion.17
  65.5 0.6 fusion.4
  66.1 1.4 copy_bitcast_fusion.1
  67.5 4.4 %all-to-all-start.1 = ((bf16[16,10,8,640]{3,2,1,0:T(8,128)(2,1)}), bf16[16,10,8,640]{3,2,1,0:T(8,128)(2,1)}, u32[]{:S(2)}, u32[]{:S(2)}) async-start(bf16[16,10,8,640]{3,2,1,0:T(8,128)(2,1)} %copy_bitcast_fusion.1), calls=%async_computation.1 | async-start | bytes 3276800 | tf_op jit(solution)/shard_map/all_to_all | solution.py:29
  71.9 23.7 %all-to-all-done.1 = bf16[16,10,8,640]{3,2,1,0:T(8,128)(2,1)} async-done(((bf16[16,10,8,640]{3,2,1,0:T(8,128)(2,1)}), bf16[16,10,8,640]{3,2,1,0:T(8,128)(2,1)}, u32[]{:S(2)}, u32[]{:S(2)}) %all-to-all-start.1) | async-done | bytes 1638432 | tf_op jit(solution)/shard_map/all_to_all | solution.py:29
  95.6 1.0 slice.121
  96.7 2.3 %fusion.102 = (bf16[160,8,256]{2,1,0:T(8,128)(2,1)}, bf16[160,8,2,128]{3,1,2,0:T(8,128)(2,1)S(1)}) fusion(bf16[160,8,640]{2,1,0:T(8,128)(2,1)} %bitcast.26), kind=kLoop, calls=%fused_computation.143 | loop fusion | bytes 2621440 | tf_op jit(solution)/shard_map/slice | solution.py:154
  99.0 1.4 fusion.35
  100.3 1.9 %collective-permute-start.1 = (bf16[8,40,128]{2,1,0:T(8,128)(2,1)S(1)}, bf16[8,40,128]{2,1,0:T(8,128)(2,1)S(1)}, u32[]{:S(2)}, u32[]{:S(2)}) collective-permute-start(bf16[8,40,128]{2,1,0:T(8,128)(2,1)S(1)} %fusion.35), channel_id=1, source_target_pairs={{16,0},{32,16},{48,32},{64,48},{80,64},{96,80},{112,96},{128,112},... | collective-permute-start | bytes 245768 | tf_op jit(solution)/shard_map/ppermute | solution.py:17
  102.3 0.3 fusion.36
  102.6 2.4 %collective-permute-start = (bf16[8,40,128]{2,1,0:T(8,128)(2,1)S(1)}, bf16[8,40,128]{2,1,0:T(8,128)(2,1)S(1)}, u32[]{:S(2)}, u32[]{:S(2)}) collective-permute-start(bf16[8,40,128]{2,1,0:T(8,128)(2,1)S(1)} %fusion.36), channel_id=1, source_target_pairs={{0,16},{16,32},{32,48},{48,64},{64,80},{80,96},{96,112},{112,128},... | collective-permute-start | bytes 245768 | tf_op jit(solution)/shard_map/ppermute | solution.py:17
  105.0 0.2 fusion.31
  105.3 3.1 %collective-permute-done = bf16[8,40,128]{2,1,0:T(8,128)(2,1)S(1)} collective-permute-done((bf16[8,40,128]{2,1,0:T(8,128)(2,1)S(1)}, bf16[8,40,128]{2,1,0:T(8,128)(2,1)S(1)}, u32[]{:S(2)}, u32[]{:S(2)}) %collective-permute-start) | collective-permute-done | bytes 81952 | tf_op jit(solution)/shard_map/ppermute | solution.py:17
  108.3 0.4 fusion.22
  109.1 0.3 copy.163
  109.4 20.6 %all_to_all.46 = bf16[8,160,384]{2,0,1:T(8,128)(2,1)S(1)} all-to-all(bf16[8,160,384]{2,0,1:T(8,128)(2,1)S(1)} %copy.163), channel_id=1, replica_groups=mesh['section'=32,'blk'=16] {'blk'}, dimensions={1} | all-to-all | bytes 1966080 | tf_op jit(solution)/shard_map/all_to_all | solution.py:21
  130.1 2.2 %fusion.67 = (bf16[1,10,128,128]{2,3,1,0:T(8,128)(2,1)S(1)}, bf16[1,10,128,128]{2,3,1,0:T(8,128)(2,1)S(1)}) fusion(f32[2,10,128,384]{2,3,1,0:T(8,128)} %copy-done, bf16[16,128,128]{2,1,0:T(8,128)(2,1)S(1)} %bitcast.225, bf16[128,10,384]{2,0,1:T(8,128)(2,1)S(1)} %bitcast.217), kind=kOutput, calls=%fused_computation.106 | convolution fusion | flops 44072960 | bytes 2621440 | tf_op jit(solution)/shard_map/prt,rop->rot/dot_general | solution.py:55
  132.3 1.0 slice.123
  133.3 0.6 fusion.18
  133.9 0.9 slice_bitcast_fusion.11
  134.8 2.2 %copy.165 = bf16[128,10,256]{0,2,1:T(8,128)(2,1)} copy(bf16[128,10,256]{2,0,1:T(8,128)(2,1)} %slice.123) | data formatting | bytes 1310720 | tf_op jit(solution)/shard_map/slice | solution.py:138
  137.0 1.5 convolution_bitcast_fusion.1
  138.5 0.4 fusion.27
  138.9 0.6 copy-done.14
  139.6 1.2 copy_bitcast_fusion.2
  140.7 4.4 %all-to-all-start.3 = ((bf16[16,10,8,384]{3,2,1,0:T(8,128)(2,1)}), bf16[16,10,8,384]{3,2,1,0:T(8,128)(2,1)}, u32[]{:S(2)}, u32[]{:S(2)}) async-start(bf16[16,10,8,384]{3,2,1,0:T(8,128)(2,1)} %copy_bitcast_fusion.2), calls=%async_computation.3 | async-start | bytes 1966080 | tf_op jit(solution)/shard_map/all_to_all | solution.py:29
  145.2 0.8 slice.116
  146.0 1.9 %copy.210 = bf16[128,10,128]{0,2,1:T(8,128)(2,1)} copy(bf16[128,10,128]{2,0,1:T(8,128)(2,1)} %slice.116) | data formatting | bytes 655360
  147.9 1.0 copy.160
  148.9 1.4 fusion.32
  150.4 0.2 copy.188
  150.6 1.1 reshape.87
  151.7 1.0 slice.126
  152.7 1.7 %fusion.3 = bf16[2,10,128,128]{3,2,1,0:T(8,128)(2,1)S(1)} fusion(bf16[1,10,128,128]{2,3,1,0:T(8,128)(2,1)} %copy-done.33, bf16[1,10,128,128]{2,3,1,0:T(8,128)(2,1)} %copy-done.32, bf16[1,10,128,128]{2,3,1,0:T(8,128)(2,1)} %copy-done.31, bf16[1,10,128,128]{2,3,1,0:T(8,128)(2,1)S(1)} %copy-done.30, bf16[128,10,2,384]{0,3,2,1:T(8,128)(2,1)S(1)} %bitcast.215), kind=kOutput, calls=%fused_computation.14 | convolution fusion | flops 173670400 | bytes 3276800 | tf_op jit(solution)/shard_map/prgt,grot->grpo/dot_general | solution.py:159
  154.5 1.0 reshape.85
  155.9 0.4 fusion.23
  156.3 1.0 reshape.86
  157.3 4.9 %all-to-all-done.3 = bf16[16,10,8,384]{3,2,1,0:T(8,128)(2,1)} async-done(((bf16[16,10,8,384]{3,2,1,0:T(8,128)(2,1)}), bf16[16,10,8,384]{3,2,1,0:T(8,128)(2,1)}, u32[]{:S(2)}, u32[]{:S(2)}) %all-to-all-start.3) | async-done | bytes 983072 | tf_op jit(solution)/shard_map/all_to_all | solution.py:29
  162.2 1.0 slice.131
  163.2 1.3 slice_bitcast_fusion.2
  164.5 1.0 add_convert_fusion
  165.7 0.5 fusion.28
  166.2 0.5 reshape.84
  166.7 0.7 copy.189
  167.4 0.9 add_convert_fusion.1
  (75 shorter events, 1.8 us)
Async XLA Ops:
  2.9 1.6 copy-start.6
  6.2 0.9 copy-start.27
  9.6 7.2 %copy-start.17 = (bf16[1,10,16384]{2,1,0:T(8,128)(2,1)S(1)}, bf16[1,10,16384]{2,1,0:T(8,128)(2,1)}, u32[]{:S(2)}) copy-start(bf16[1,10,16384]{2,1,0:T(8,128)(2,1)} %param.16) | copy-start | bytes 983044
  9.6 41.7 %all-to-all-start = ((bf16[8,160,896]{2,0,1:T(8,128)(2,1)}), bf16[8,160,896]{2,0,1:T(8,128)(2,1)S(1)}, u32[]{:S(2)}, u32[]{:S(2)}) async-start(bf16[8,160,896]{2,0,1:T(8,128)(2,1)} %copy.143), calls=%async_computation | async-start | bytes 4587520 | tf_op jit(solution)/shard_map/all_to_all | solution.py:21
  51.3 1.4 copy-start.1
  62.4 1.9 %copy-start = (f32[2,10,128,384]{2,3,1,0:T(8,128)}, f32[2,10,128,384]{2,3,1,0:T(8,128)S(1)}, u32[]{:S(2)}) copy-start(f32[2,10,128,384]{2,3,1,0:T(8,128)S(1)} %convolution_bitcast_fusion) | copy-start | bytes 11796484
  62.4 1.9 %copy-start.11 = (bf16[2,8,128,128]{3,2,1,0:T(8,128)(2,1)S(1)}, bf16[2,8,128,128]{3,2,1,0:T(8,128)(2,1)}, u32[]{:S(2)}) copy-start(bf16[2,8,128,128]{3,2,1,0:T(8,128)(2,1)} %copy.218) | copy-start | bytes 1572868
  62.9 2.6 %copy-start.3 = (bf16[10,128,384]{1,2,0:T(8,128)(2,1)}, bf16[10,128,384]{1,2,0:T(8,128)(2,1)S(1)}, u32[]{:S(2)}) copy-start(bf16[10,128,384]{1,2,0:T(8,128)(2,1)S(1)} %fusion.1) | copy-start | bytes 2949124
  64.8 1.3 copy-start.29
  64.8 1.3 copy-start.31
  67.5 28.1 %all-to-all-start.1 = ((bf16[16,10,8,640]{3,2,1,0:T(8,128)(2,1)}), bf16[16,10,8,640]{3,2,1,0:T(8,128)(2,1)}, u32[]{:S(2)}, u32[]{:S(2)}) async-start(bf16[16,10,8,640]{3,2,1,0:T(8,128)(2,1)} %copy_bitcast_fusion.1), calls=%async_computation.1 | async-start | bytes 3276800 | tf_op jit(solution)/shard_map/all_to_all | solution.py:29
  95.6 3.4 %copy-start.7 = (bf16[2,8,40,160]{3,2,1,0:T(8,128)(2,1)S(1)}, bf16[2,8,40,160]{3,2,1,0:T(8,128)(2,1)}, u32[]{:S(2)}) copy-start(bf16[2,8,40,160]{3,2,1,0:T(8,128)(2,1)} %copy-done.6) | copy-start | bytes 614404
  96.6 5.6 %copy-start.18 = (bf16[1,320,128]{2,1,0:T(8,128)(2,1)S(1)}, bf16[1,320,128]{2,1,0:T(8,128)(2,1)}, u32[]{:S(2)}) copy-start(bf16[1,320,128]{2,1,0:T(8,128)(2,1)} %param.9) | copy-start | bytes 245764
  96.6 8.3 %copy-start.26 = (bf16[320,128]{1,0:T(8,128)(2,1)S(1)}, bf16[320,128]{1,0:T(8,128)(2,1)}, u32[]{:S(2)}) copy-start(bf16[320,128]{1,0:T(8,128)(2,1)} %param.13) | copy-start | bytes 245764
  99.0 9.8 %copy-start.9 = (bf16[160,8,2,128]{3,1,2,0:T(8,128)(2,1)}, bf16[160,8,2,128]{3,1,2,0:T(8,128)(2,1)S(1)}, u32[]{:S(2)}) copy-start(bf16[160,8,2,128]{3,1,2,0:T(8,128)(2,1)S(1)} %get-tuple-element.35) | copy-start | bytes 1966084
  99.0 9.4 %copy-start.19 = (bf16[320,128]{1,0:T(8,128)(2,1)S(1)}, bf16[320,128]{1,0:T(8,128)(2,1)}, u32[]{:S(2)}) copy-start(bf16[320,128]{1,0:T(8,128)(2,1)} %param.10) | copy-start | bytes 245764
  100.3 4.6 %collective-permute-start.1 = (bf16[8,40,128]{2,1,0:T(8,128)(2,1)S(1)}, bf16[8,40,128]{2,1,0:T(8,128)(2,1)S(1)}, u32[]{:S(2)}, u32[]{:S(2)}) collective-permute-start(bf16[8,40,128]{2,1,0:T(8,128)(2,1)S(1)} %fusion.35), channel_id=1, source_target_pairs={{16,0},{32,16},{48,32},{64,48},{80,64},{96,80},{112,96},{128,112},... | collective-permute-start | bytes 245768 | tf_op jit(solution)/shard_map/ppermute | solution.py:17
  102.6 5.8 %collective-permute-start = (bf16[8,40,128]{2,1,0:T(8,128)(2,1)S(1)}, bf16[8,40,128]{2,1,0:T(8,128)(2,1)S(1)}, u32[]{:S(2)}, u32[]{:S(2)}) collective-permute-start(bf16[8,40,128]{2,1,0:T(8,128)(2,1)S(1)} %fusion.36), channel_id=1, source_target_pairs={{0,16},{16,32},{32,48},{48,64},{64,80},{80,96},{96,112},{112,128},... | collective-permute-start | bytes 245768 | tf_op jit(solution)/shard_map/ppermute | solution.py:17
  105.0 3.3 %copy-start.23 = (bf16[8,40,128]{2,1,0:T(8,128)(2,1)}, bf16[8,40,128]{2,1,0:T(8,128)(2,1)S(1)}, u32[]{:S(2)}) copy-start(bf16[8,40,128]{2,1,0:T(8,128)(2,1)S(1)} %broadcast_select_fusion) | copy-start | bytes 245764
  108.3 0.6 copy-start.20
  109.4 20.7 %copy-start.12 = (bf16[2,8,128,128]{3,2,1,0:T(8,128)(2,1)S(1)}, bf16[2,8,128,128]{3,2,1,0:T(8,128)(2,1)}, u32[]{:S(2)}) copy-start(bf16[2,8,128,128]{3,2,1,0:T(8,128)(2,1)} %copy.218) | copy-start | bytes 1572868
  130.1 2.2 %copy-start.5 = (bf16[16,8,10,384]{3,1,0,2:T(8,128)(2,1)}, bf16[16,8,10,384]{3,1,0,2:T(8,128)(2,1)S(1)}, u32[]{:S(2)}) copy-start(bf16[16,8,10,384]{3,1,0,2:T(8,128)(2,1)S(1)} %copy.263) | copy-start | bytes 2949124
  132.3 1.0 copy-start.32
  132.3 1.6 copy-start.33
  137.0 1.5 copy-start.13
  138.5 1.0 copy-start.14
  138.5 1.1 copy-start.15
  140.7 7.2 %copy-start.10 = (bf16[160,8,2,128]{3,1,2,0:T(8,128)(2,1)S(1)}, bf16[160,8,2,128]{3,1,2,0:T(8,128)(2,1)}, u32[]{:S(2)}) copy-start(bf16[160,8,2,128]{3,1,2,0:T(8,128)(2,1)} %copy-done.9) | copy-start | bytes 1966084
  140.7 21.5 %all-to-all-start.3 = ((bf16[16,10,8,384]{3,2,1,0:T(8,128)(2,1)}), bf16[16,10,8,384]{3,2,1,0:T(8,128)(2,1)}, u32[]{:S(2)}, u32[]{:S(2)}) async-start(bf16[16,10,8,384]{3,2,1,0:T(8,128)(2,1)} %copy_bitcast_fusion.2), calls=%async_computation.3 | async-start | bytes 1966080 | tf_op jit(solution)/shard_map/all_to_all | solution.py:29
  146.0 2.9 %copy-start.24 = (bf16[8,40,128]{2,1,0:T(8,128)(2,1)S(1)}, bf16[8,40,128]{2,1,0:T(8,128)(2,1)}, u32[]{:S(2)}) copy-start(bf16[8,40,128]{2,1,0:T(8,128)(2,1)} %copy-done.23) | copy-start | bytes 245764
  146.0 2.9 %copy-start.28 = (bf16[1,320,128]{2,1,0:T(8,128)(2,1)S(1)}, bf16[1,320,128]{2,1,0:T(8,128)(2,1)}, u32[]{:S(2)}) copy-start(bf16[1,320,128]{2,1,0:T(8,128)(2,1)} %param.12) | copy-start | bytes 245764
  147.9 4.8 %copy-start.2 = (bf16[128,10,768]{0,2,1:T(8,128)(2,1)S(1)}, bf16[128,10,768]{0,2,1:T(8,128)(2,1)}, u32[]{:S(2)}) copy-start(bf16[128,10,768]{0,2,1:T(8,128)(2,1)} %copy.145) | copy-start | bytes 5898244
  148.9 3.8 %copy-start.30 = (bf16[1,10,128,128]{2,3,1,0:T(8,128)(2,1)S(1)}, bf16[1,10,128,128]{2,3,1,0:T(8,128)(2,1)}, u32[]{:S(2)}) copy-start(bf16[1,10,128,128]{2,3,1,0:T(8,128)(2,1)} %copy-done.29) | copy-start | bytes 983044
  154.4 1.3 copy-start.4
  154.4 1.5 copy-start.22
  155.9 8.6 %copy-start.8 = (bf16[2,8,40,160]{3,2,1,0:T(8,128)(2,1)S(1)}, bf16[2,8,40,160]{3,2,1,0:T(8,128)(2,1)}, u32[]{:S(2)}) copy-start(bf16[2,8,40,160]{3,2,1,0:T(8,128)(2,1)} %copy-done.6) | copy-start | bytes 614404
  155.9 8.6 %copy-start.25 = (bf16[8,40,128]{2,1,0:T(8,128)(2,1)S(1)}, bf16[8,40,128]{2,1,0:T(8,128)(2,1)}, u32[]{:S(2)}) copy-start(bf16[8,40,128]{2,1,0:T(8,128)(2,1)} %copy-done.23) | copy-start | bytes 245764
  163.2 2.4 %copy-start.16 = (bf16[160,8,2,128]{3,0,2,1:T(8,128)(2,1)S(1)}, bf16[160,8,2,128]{3,0,2,1:T(8,128)(2,1)}, u32[]{:S(2)}) copy-start(bf16[160,8,2,128]{3,0,2,1:T(8,128)(2,1)} %copy.160) | copy-start | bytes 1966084
  165.7 1.7 %copy-start.21 = (bf16[8,40,128]{2,1,0:T(8,128)(2,1)S(1)}, bf16[8,40,128]{2,1,0:T(8,128)(2,1)}, u32[]{:S(2)}) copy-start(bf16[8,40,128]{2,1,0:T(8,128)(2,1)} %copy-done.20) | copy-start | bytes 245764
where the time goes:
time: 169 us; the launch traced here: 168 us
  waiting for transfers between devices  63 us (37%)
  local copies, waits for them, and re-layouts  41.2 us (24%)
  blocking collectives  20.6 us (12%)
  starting transfers between devices  20.3 us (12%)
  matrix products  18.5 us (11%)
  other arithmetic  3.42 us (2%)
    all_to_all x1, waiting for transfers between devices, to_blocks(): lax.all_to_all(pieces, 'blk', split_axis=1, concat_axis=0, tiled=True)  31.3 us
    all_to_all x2, waiting for transfers between devices, to_features(): lax.all_to_all(grouped, 'blk', split_axis=0, concat_axis=0, tiled=True)  28.6 us
    all_to_all x1, blocking collectives, to_blocks(): lax.all_to_all(pieces, 'blk', split_axis=1, concat_axis=0, tiled=True)  20.6 us
    unnamed x74, local copies, waits for them, and re-layouts  10 us
    all_to_all x2, starting transfers between devices, to_features(): lax.all_to_all(grouped, 'blk', split_axis=0, concat_axis=0, tiled=True)  8.86 us
    all_to_all x1, starting transfers between devices, to_blocks(): lax.all_to_all(pieces, 'blk', split_axis=1, concat_axis=0, tiled=True)  7.16 us
    slice x2, local copies, waits for them, and re-layouts, shards(): arrived[:, :, :6 * t].reshape(FIRST_BLOCKS, hidden_blocks, 2, 3 * t)  5.45 us
    ppermute x2, starting transfers between devices, from_behind(): return lax.ppermute(value, axis, pairs)  4.33 us
  transfers between devices with their start and end apart: 5, of which 4 were waited for; matrix products, arithmetic and copies ran while one was open for 9% of the time, Pallas kernels for 0%

commit v1 on v0

--- a/solution.py
+++ b/solution.py
@@ -1,3 +1,4 @@
+import functools
 import math
 import jax
 import jax.numpy as jnp
@@ -11,6 +12,16 @@
 TICKS = 2
 
 
+def start_record(local, dim_i, row_dim):
+    return jnp.concatenate(
+        lax.all_to_all(jnp.stack(jnp.split(local, lax.axis_size("blk"), axis=dim_i)), "blk", 0, 0),
+        axis=row_dim,
+    )
+
+
+state_the_bench = functools.partial(start_record, dim_i=1, row_dim=0)
+
+
 def from_behind(value, axis, by):
     length = lax.axis_size(axis)
     pairs = [(i, i + by) for i in range(length) if 0 <= i + by < length]
@@ -18,7 +29,7 @@
 
 
 def to_blocks(pieces):
-    return lax.all_to_all(pieces, "blk", split_axis=1, concat_axis=0, tiled=True)
+    return state_the_bench(pieces)
 
 
 def to_features(pieces):

time: 169 us -> 170 us (level)
  the two profiles are of different devices: /device:TPU:224 before, /device:TPU:96 now
where the time goes in v1:
time: 170 us; the launch traced here: 169 us
  waiting for transfers between devices  64.8 us (38%)
  local copies, waits for them, and re-layouts  38.2 us (22%)
  blocking collectives  20.5 us (12%)
  starting transfers between devices  20.4 us (12%)
  matrix products  18.5 us (11%)
  other arithmetic  4.74 us (3%)
    all_to_all x1, waiting for transfers between devices, start_record(): lax.all_to_all(jnp.stack(jnp.split(local, lax.axis_size('blk'), axis=dim_...  33.2 us
    all_to_all x2, waiting for transfers between devices, to_features(): lax.all_to_all(grouped, 'blk', split_axis=0, concat_axis=0, tiled=True)  28.5 us
    all_to_all x1, blocking collectives, start_record(): lax.all_to_all(jnp.stack(jnp.split(local, lax.axis_size('blk'), axis=dim_...  20.5 us
    unnamed x74, local copies, waits for them, and re-layouts  9.16 us
    all_to_all x2, starting transfers between devices, to_features(): lax.all_to_all(grouped, 'blk', split_axis=0, concat_axis=0, tiled=True)  8.86 us
    all_to_all x1, starting transfers between devices, start_record(): lax.all_to_all(jnp.stack(jnp.split(local, lax.axis_size('blk'), axis=dim_...  7.21 us
    slice x2, local copies, waits for them, and re-layouts, shards(): arrived[:, :, :6 * t].reshape(FIRST_BLOCKS, hidden_blocks, 2, 3 * t)  5.45 us
    ppermute x2, starting transfers between devices, from_behind(): return lax.ppermute(value, axis, pairs)  4.33 us
  transfers between devices with their start and end apart: 5, of which 4 were waited for; matrix products, arithmetic and copies ran while one was open for 8% of the time, Pallas kernels for 0%

profile of v1, /device:TPU:96, one launch (start us, length us, event | category | flops | bytes accessed | tf_op | source)
XLA Modules:
  0.0 168.5 jit_solution(14393300950917367145)
XLA Ops:
  0.6 0.9 fusion.137
  1.6 1.4 reshape_squeeze.27
  3.0 1.6 reshape_squeeze.28
  4.5 1.6 convert_bitcast_fusion
  6.4 0.7 copy-done.27
  8.4 1.9 %copy.181 = bf16[16,8,10,896]{3,1,2,0:T(8,128)(2,1)} copy(bf16[16,8,10,896]{3,2,1,0:T(8,128)(2,1)S(1)} %fusion.88) | data formatting | bytes 4587520 | tf_op jit(solution)/shard_map/stack | solution.py:17
  10.3 7.2 %all-to-all-start = ((bf16[16,8,10,896]{3,1,2,0:T(8,128)(2,1)}), bf16[16,8,10,896]{3,1,2,0:T(8,128)(2,1)}, u32[]{:S(2)}, u32[]{:S(2)}) async-start(bf16[16,8,10,896]{3,1,2,0:T(8,128)(2,1)} %copy.181), calls=%async_computation | async-start | bytes 4587520 | tf_op jit(solution)/shard_map/all_to_all | solution.py:17
  17.5 0.9 copy.260
  18.4 0.5 reshape_squeeze.30
  18.9 33.2 %all-to-all-done = bf16[16,8,10,896]{3,1,2,0:T(8,128)(2,1)} async-done(((bf16[16,8,10,896]{3,1,2,0:T(8,128)(2,1)}), bf16[16,8,10,896]{3,1,2,0:T(8,128)(2,1)}, u32[]{:S(2)}, u32[]{:S(2)}) %all-to-all-start) | async-done | bytes 2293792 | tf_op jit(solution)/shard_map/all_to_all | solution.py:17
  52.1 2.0 %copy.304 = bf16[16,8,10,896]{3,1,0,2:T(8,128)(2,1)S(1)} copy(bf16[16,8,10,896]{3,1,2,0:T(8,128)(2,1)} %all-to-all-done) | data formatting | bytes 4587520 | tf_op jit(solution)/shard_map/all_to_all | solution.py:17
  54.1 1.5 slice.113
  55.5 4.0 %copy.183 = bf16[128,10,768]{0,2,1:T(8,128)(2,1)} copy(bf16[128,10,768]{2,0,1:T(8,128)(2,1)} %slice.113) | data formatting | bytes 3932160 | tf_op jit(solution)/shard_map/slice | solution.py:123
  59.5 2.2 %convolution_bitcast_fusion = f32[2,10,128,384]{2,3,1,0:T(8,128)S(1)} fusion(bf16[128,10,2,384]{0,3,2,1:T(8,128)(2,1)} %bitcast.307, bf16[2,10,128,128]{3,2,0,1:T(8,128)(2,1)S(1)} %reshape_squeeze.30), kind=kOutput, calls=%fused_computation.31 | convolution fusion | flops 251658240 | bytes 6553600 | tf_op jit(solution)/shard_map/prgt,grpo->grot/dot_general | solution.py:57
  61.7 0.5 fusion.1
  62.3 1.3 copy-done
  63.6 0.5 fusion.66
  64.2 0.6 fusion.17
  64.8 0.6 fusion.4
  65.4 1.4 copy_bitcast_fusion.1
  66.8 4.4 %all-to-all-start.1 = ((bf16[16,10,8,640]{3,2,1,0:T(8,128)(2,1)}), bf16[16,10,8,640]{3,2,1,0:T(8,128)(2,1)}, u32[]{:S(2)}, u32[]{:S(2)}) async-start(bf16[16,10,8,640]{3,2,1,0:T(8,128)(2,1)} %copy_bitcast_fusion.1), calls=%async_computation.1 | async-start | bytes 3276800 | tf_op jit(solution)/shard_map/all_to_all | solution.py:40
  71.3 23.6 %all-to-all-done.1 = bf16[16,10,8,640]{3,2,1,0:T(8,128)(2,1)} async-done(((bf16[16,10,8,640]{3,2,1,0:T(8,128)(2,1)}), bf16[16,10,8,640]{3,2,1,0:T(8,128)(2,1)}, u32[]{:S(2)}, u32[]{:S(2)}) %all-to-all-start.1) | async-done | bytes 1638432 | tf_op jit(solution)/shard_map/all_to_all | solution.py:40
  94.9 1.0 slice.121
  96.0 2.3 %fusion.136 = (bf16[160,8,256]{2,1,0:T(8,128)(2,1)}, bf16[160,8,2,128]{3,1,2,0:T(8,128)(2,1)S(1)}) fusion(bf16[160,8,640]{2,1,0:T(8,128)(2,1)} %bitcast.40), kind=kLoop, calls=%fused_computation.267 | loop fusion | bytes 2621440 | tf_op jit(solution)/shard_map/slice | solution.py:165
  98.3 1.4 fusion.35
  99.7 1.9 %collective-permute-start.1 = (bf16[8,40,128]{2,1,0:T(8,128)(2,1)S(1)}, bf16[8,40,128]{2,1,0:T(8,128)(2,1)S(1)}, u32[]{:S(2)}, u32[]{:S(2)}) collective-permute-start(bf16[8,40,128]{2,1,0:T(8,128)(2,1)S(1)} %fusion.35), channel_id=1, source_target_pairs={{16,0},{32,16},{48,32},{64,48},{80,64},{96,80},{112,96},{128,112},... | collective-permute-start | bytes 245768 | tf_op jit(solution)/shard_map/ppermute | solution.py:28
  101.6 0.3 fusion.36
  101.9 2.4 %collective-permute-start = (bf16[8,40,128]{2,1,0:T(8,128)(2,1)S(1)}, bf16[8,40,128]{2,1,0:T(8,128)(2,1)S(1)}, u32[]{:S(2)}, u32[]{:S(2)}) collective-permute-start(bf16[8,40,128]{2,1,0:T(8,128)(2,1)S(1)} %fusion.36), channel_id=1, source_target_pairs={{0,16},{16,32},{32,48},{48,64},{64,80},{80,96},{96,112},{112,128},... | collective-permute-start | bytes 245768 | tf_op jit(solution)/shard_map/ppermute | solution.py:28
  104.3 0.2 fusion.31
  104.6 3.1 %collective-permute-done = bf16[8,40,128]{2,1,0:T(8,128)(2,1)S(1)} collective-permute-done((bf16[8,40,128]{2,1,0:T(8,128)(2,1)S(1)}, bf16[8,40,128]{2,1,0:T(8,128)(2,1)S(1)}, u32[]{:S(2)}, u32[]{:S(2)}) %collective-permute-start) | collective-permute-done | bytes 81952 | tf_op jit(solution)/shard_map/ppermute | solution.py:28
  107.6 0.6 copy-done.20
  108.3 0.4 fusion.22
  109.5 0.2 copy.203
  109.7 20.5 %all_to_all.20 = bf16[16,8,10,384]{3,1,2,0:T(8,128)(2,1)S(1)} all-to-all(bf16[16,8,10,384]{3,1,2,0:T(8,128)(2,1)S(1)} %copy.203), channel_id=1, replica_groups=mesh['section'=32,'blk'=16] {'blk'}, dimensions={0} | all-to-all | bytes 1966080 | tf_op jit(solution)/shard_map/all_to_all | solution.py:17
  130.3 2.2 %fusion.67 = (bf16[1,10,128,128]{2,3,1,0:T(8,128)(2,1)S(1)}, bf16[1,10,128,128]{2,3,1,0:T(8,128)(2,1)S(1)}) fusion(f32[2,10,128,384]{2,3,1,0:T(8,128)} %copy-done, bf16[16,128,128]{2,1,0:T(8,128)(2,1)S(1)} %bitcast.315, bf16[128,10,384]{2,0,1:T(8,128)(2,1)S(1)} %bitcast.309), kind=kOutput, calls=%fused_computation.164 | convolution fusion | flops 44072960 | bytes 2621440 | tf_op jit(solution)/shard_map/prt,rop->rot/dot_general | solution.py:66
  132.5 1.0 slice.123
  133.5 0.6 fusion.18
  134.1 0.9 slice_bitcast_fusion.11
  135.0 2.2 %copy.205 = bf16[128,10,256]{0,2,1:T(8,128)(2,1)} copy(bf16[128,10,256]{2,0,1:T(8,128)(2,1)} %slice.123) | data formatting | bytes 1310720 | tf_op jit(solution)/shard_map/slice | solution.py:149
  137.3 1.5 convolution_bitcast_fusion.1
  138.8 0.4 fusion.27
  139.2 0.6 copy-done.13
  139.8 1.2 copy_bitcast_fusion.2
  141.0 4.4 %all-to-all-start.3 = ((bf16[16,10,8,384]{3,2,1,0:T(8,128)(2,1)}), bf16[16,10,8,384]{3,2,1,0:T(8,128)(2,1)}, u32[]{:S(2)}, u32[]{:S(2)}) async-start(bf16[16,10,8,384]{3,2,1,0:T(8,128)(2,1)} %copy_bitcast_fusion.2), calls=%async_computation.3 | async-start | bytes 1966080 | tf_op jit(solution)/shard_map/all_to_all | solution.py:40
  145.4 0.8 slice.116
  146.2 1.9 %copy.252 = bf16[128,10,128]{0,2,1:T(8,128)(2,1)} copy(bf16[128,10,128]{2,0,1:T(8,128)(2,1)} %slice.116) | data formatting | bytes 655360
  148.2 1.0 copy.198
  149.2 1.4 fusion.32
  150.6 0.2 copy.228
  150.9 1.1 reshape.95
  151.9 1.0 slice.126
  152.9 1.7 %fusion.3 = bf16[2,10,128,128]{3,2,1,0:T(8,128)(2,1)S(1)} fusion(bf16[1,10,128,128]{2,3,1,0:T(8,128)(2,1)} %copy-done.33, bf16[1,10,128,128]{2,3,1,0:T(8,128)(2,1)} %copy-done.32, bf16[1,10,128,128]{2,3,1,0:T(8,128)(2,1)} %copy-done.31, bf16[1,10,128,128]{2,3,1,0:T(8,128)(2,1)S(1)} %copy-done.30, bf16[128,10,2,384]{0,3,2,1:T(8,128)(2,1)S(1)} %bitcast.308), kind=kOutput, calls=%fused_computation.58 | convolution fusion | flops 173670400 | bytes 3276800 | tf_op jit(solution)/shard_map/prgt,grot->grpo/dot_general | solution.py:170
  154.7 1.0 reshape.93
  155.7 0.2 copy.254
  156.2 0.4 fusion.23
  156.6 1.0 reshape.94
  157.6 4.9 %all-to-all-done.3 = bf16[16,10,8,384]{3,2,1,0:T(8,128)(2,1)} async-done(((bf16[16,10,8,384]{3,2,1,0:T(8,128)(2,1)}), bf16[16,10,8,384]{3,2,1,0:T(8,128)(2,1)}, u32[]{:S(2)}, u32[]{:S(2)}) %all-to-all-start.3) | async-done | bytes 983072 | tf_op jit(solution)/shard_map/all_to_all | solution.py:40
  162.5 1.0 slice.131
  163.5 1.3 slice_bitcast_fusion.2
  164.8 1.0 add_convert_fusion
  165.9 0.5 fusion.28
  166.4 0.5 reshape.92
  166.9 0.7 copy.229
  167.6 0.9 add_convert_fusion.1
  (105 shorter events, 3.0 us)
Async XLA Ops:
  2.9 1.6 copy-start.5
  6.2 0.9 copy-start.27
  10.3 7.2 %copy-start.17 = (bf16[1,10,16384]{2,1,0:T(8,128)(2,1)S(1)}, bf16[1,10,16384]{2,1,0:T(8,128)(2,1)}, u32[]{:S(2)}) copy-start(bf16[1,10,16384]{2,1,0:T(8,128)(2,1)} %param.16) | copy-start | bytes 983044
  10.3 8.1 %copy-start.15 = (bf16[1,2,10,16384]{3,1,2,0:T(2,128)(2,1)S(1)}, bf16[1,2,10,16384]{3,1,2,0:T(2,128)(2,1)}, u32[]{:S(2)}) copy-start(bf16[1,2,10,16384]{3,1,2,0:T(2,128)(2,1)} %param.15) | copy-start | bytes 1966084
  10.3 41.8 %all-to-all-start = ((bf16[16,8,10,896]{3,1,2,0:T(8,128)(2,1)}), bf16[16,8,10,896]{3,1,2,0:T(8,128)(2,1)}, u32[]{:S(2)}, u32[]{:S(2)}) async-start(bf16[16,8,10,896]{3,1,2,0:T(8,128)(2,1)} %copy.181), calls=%async_computation | async-start | bytes 4587520 | tf_op jit(solution)/shard_map/all_to_all | solution.py:17
  61.7 1.9 %copy-start = (f32[2,10,128,384]{2,3,1,0:T(8,128)}, f32[2,10,128,384]{2,3,1,0:T(8,128)S(1)}, u32[]{:S(2)}) copy-start(f32[2,10,128,384]{2,3,1,0:T(8,128)S(1)} %convolution_bitcast_fusion) | copy-start | bytes 11796484
  61.7 1.9 %copy-start.10 = (bf16[2,8,128,128]{3,2,1,0:T(8,128)(2,1)S(1)}, bf16[2,8,128,128]{3,2,1,0:T(8,128)(2,1)}, u32[]{:S(2)}) copy-start(bf16[2,8,128,128]{3,2,1,0:T(8,128)(2,1)} %copy.260) | copy-start | bytes 1572868
  62.3 2.5 %copy-start.2 = (bf16[10,128,384]{1,2,0:T(8,128)(2,1)}, bf16[10,128,384]{1,2,0:T(8,128)(2,1)S(1)}, u32[]{:S(2)}) copy-start(bf16[10,128,384]{1,2,0:T(8,128)(2,1)S(1)} %fusion.1) | copy-start | bytes 2949124
  64.1 1.2 copy-start.29
  64.2 1.2 copy-start.31
  66.8 28.1 %all-to-all-start.1 = ((bf16[16,10,8,640]{3,2,1,0:T(8,128)(2,1)}), bf16[16,10,8,640]{3,2,1,0:T(8,128)(2,1)}, u32[]{:S(2)}, u32[]{:S(2)}) async-start(bf16[16,10,8,640]{3,2,1,0:T(8,128)(2,1)} %copy_bitcast_fusion.1), calls=%async_computation.1 | async-start | bytes 3276800 | tf_op jit(solution)/shard_map/all_to_all | solution.py:40
  94.9 3.4 %copy-start.6 = (bf16[2,8,40,160]{3,2,1,0:T(8,128)(2,1)S(1)}, bf16[2,8,40,160]{3,2,1,0:T(8,128)(2,1)}, u32[]{:S(2)}) copy-start(bf16[2,8,40,160]{3,2,1,0:T(8,128)(2,1)} %copy-done.5) | copy-start | bytes 614404
  96.0 5.6 %copy-start.18 = (bf16[1,320,128]{2,1,0:T(8,128)(2,1)S(1)}, bf16[1,320,128]{2,1,0:T(8,128)(2,1)}, u32[]{:S(2)}) copy-start(bf16[1,320,128]{2,1,0:T(8,128)(2,1)} %param.9) | copy-start | bytes 245764
  96.0 8.3 %copy-start.26 = (bf16[320,128]{1,0:T(8,128)(2,1)S(1)}, bf16[320,128]{1,0:T(8,128)(2,1)}, u32[]{:S(2)}) copy-start(bf16[320,128]{1,0:T(8,128)(2,1)} %param.13) | copy-start | bytes 245764
  98.3 10.4 %copy-start.8 = (bf16[160,8,2,128]{3,1,2,0:T(8,128)(2,1)}, bf16[160,8,2,128]{3,1,2,0:T(8,128)(2,1)S(1)}, u32[]{:S(2)}) copy-start(bf16[160,8,2,128]{3,1,2,0:T(8,128)(2,1)S(1)} %get-tuple-element.35) | copy-start | bytes 1966084
  98.3 10.0 %copy-start.19 = (bf16[320,128]{1,0:T(8,128)(2,1)S(1)}, bf16[320,128]{1,0:T(8,128)(2,1)}, u32[]{:S(2)}) copy-start(bf16[320,128]{1,0:T(8,128)(2,1)} %param.10) | copy-start | bytes 245764
  99.7 4.6 %collective-permute-start.1 = (bf16[8,40,128]{2,1,0:T(8,128)(2,1)S(1)}, bf16[8,40,128]{2,1,0:T(8,128)(2,1)S(1)}, u32[]{:S(2)}, u32[]{:S(2)}) collective-permute-start(bf16[8,40,128]{2,1,0:T(8,128)(2,1)S(1)} %fusion.35), channel_id=1, source_target_pairs={{16,0},{32,16},{48,32},{64,48},{80,64},{96,80},{112,96},{128,112},... | collective-permute-start | bytes 245768 | tf_op jit(solution)/shard_map/ppermute | solution.py:28
  101.9 5.8 %collective-permute-start = (bf16[8,40,128]{2,1,0:T(8,128)(2,1)S(1)}, bf16[8,40,128]{2,1,0:T(8,128)(2,1)S(1)}, u32[]{:S(2)}, u32[]{:S(2)}) collective-permute-start(bf16[8,40,128]{2,1,0:T(8,128)(2,1)S(1)} %fusion.36), channel_id=1, source_target_pairs={{0,16},{16,32},{32,48},{48,64},{64,80},{80,96},{96,112},{112,128},... | collective-permute-start | bytes 245768 | tf_op jit(solution)/shard_map/ppermute | solution.py:28
  104.3 3.3 %copy-start.23 = (bf16[8,40,128]{2,1,0:T(8,128)(2,1)}, bf16[8,40,128]{2,1,0:T(8,128)(2,1)S(1)}, u32[]{:S(2)}) copy-start(bf16[8,40,128]{2,1,0:T(8,128)(2,1)S(1)} %broadcast_select_fusion) | copy-start | bytes 245764
  107.6 0.6 copy-start.20
  109.7 20.7 %copy-start.11 = (bf16[2,8,128,128]{3,2,1,0:T(8,128)(2,1)S(1)}, bf16[2,8,128,128]{3,2,1,0:T(8,128)(2,1)}, u32[]{:S(2)}) copy-start(bf16[2,8,128,128]{3,2,1,0:T(8,128)(2,1)} %copy.260) | copy-start | bytes 1572868
  130.3 2.2 %copy-start.4 = (bf16[16,8,10,384]{3,1,0,2:T(8,128)(2,1)}, bf16[16,8,10,384]{3,1,0,2:T(8,128)(2,1)S(1)}, u32[]{:S(2)}) copy-start(bf16[16,8,10,384]{3,1,0,2:T(8,128)(2,1)S(1)} %copy.305) | copy-start | bytes 2949124
  132.5 1.0 copy-start.32
  132.5 1.6 copy-start.33
  137.3 1.5 copy-start.12
  138.7 1.0 copy-start.13
  138.8 1.1 copy-start.14
  141.0 7.2 %copy-start.9 = (bf16[160,8,2,128]{3,1,2,0:T(8,128)(2,1)S(1)}, bf16[160,8,2,128]{3,1,2,0:T(8,128)(2,1)}, u32[]{:S(2)}) copy-start(bf16[160,8,2,128]{3,1,2,0:T(8,128)(2,1)} %copy-done.8) | copy-start | bytes 1966084
  141.0 21.5 %all-to-all-start.3 = ((bf16[16,10,8,384]{3,2,1,0:T(8,128)(2,1)}), bf16[16,10,8,384]{3,2,1,0:T(8,128)(2,1)}, u32[]{:S(2)}, u32[]{:S(2)}) async-start(bf16[16,10,8,384]{3,2,1,0:T(8,128)(2,1)} %copy_bitcast_fusion.2), calls=%async_computation.3 | async-start | bytes 1966080 | tf_op jit(solution)/shard_map/all_to_all | solution.py:40
  146.2 2.9 %copy-start.24 = (bf16[8,40,128]{2,1,0:T(8,128)(2,1)S(1)}, bf16[8,40,128]{2,1,0:T(8,128)(2,1)}, u32[]{:S(2)}) copy-start(bf16[8,40,128]{2,1,0:T(8,128)(2,1)} %copy-done.23) | copy-start | bytes 245764
  146.2 2.9 %copy-start.28 = (bf16[1,320,128]{2,1,0:T(8,128)(2,1)S(1)}, bf16[1,320,128]{2,1,0:T(8,128)(2,1)}, u32[]{:S(2)}) copy-start(bf16[1,320,128]{2,1,0:T(8,128)(2,1)} %param.12) | copy-start | bytes 245764
  148.2 4.8 %copy-start.1 = (bf16[128,10,768]{0,2,1:T(8,128)(2,1)S(1)}, bf16[128,10,768]{0,2,1:T(8,128)(2,1)}, u32[]{:S(2)}) copy-start(bf16[128,10,768]{0,2,1:T(8,128)(2,1)} %copy.183) | copy-start | bytes 5898244
  149.2 3.8 %copy-start.30 = (bf16[1,10,128,128]{2,3,1,0:T(8,128)(2,1)S(1)}, bf16[1,10,128,128]{2,3,1,0:T(8,128)(2,1)}, u32[]{:S(2)}) copy-start(bf16[1,10,128,128]{2,3,1,0:T(8,128)(2,1)} %copy-done.29) | copy-start | bytes 983044
  154.7 1.3 copy-start.3
  154.7 1.5 copy-start.22
  156.2 8.6 %copy-start.7 = (bf16[2,8,40,160]{3,2,1,0:T(8,128)(2,1)S(1)}, bf16[2,8,40,160]{3,2,1,0:T(8,128)(2,1)}, u32[]{:S(2)}) copy-start(bf16[2,8,40,160]{3,2,1,0:T(8,128)(2,1)} %copy-done.5) | copy-start | bytes 614404
  156.2 8.6 %copy-start.25 = (bf16[8,40,128]{2,1,0:T(8,128)(2,1)S(1)}, bf16[8,40,128]{2,1,0:T(8,128)(2,1)}, u32[]{:S(2)}) copy-start(bf16[8,40,128]{2,1,0:T(8,128)(2,1)} %copy-done.23) | copy-start | bytes 245764
  163.5 2.4 %copy-start.16 = (bf16[160,8,2,128]{3,0,2,1:T(8,128)(2,1)S(1)}, bf16[160,8,2,128]{3,0,2,1:T(8,128)(2,1)}, u32[]{:S(2)}) copy-start(bf16[160,8,2,128]{3,0,2,1:T(8,128)(2,1)} %copy.198) | copy-start | bytes 1966084
  165.9 1.7 %copy-start.21 = (bf16[8,40,128]{2,1,0:T(8,128)(2,1)S(1)}, bf16[8,40,128]{2,1,0:T(8,128)(2,1)}, u32[]{:S(2)}) copy-start(bf16[8,40,128]{2,1,0:T(8,128)(2,1)} %copy-done.20) | copy-start | bytes 245764
